TPU v7x, 32 devices: a whole 2x2x4 slice. The times are simulated.
32 devices in a mesh: groups: 2 (over y), ctx: 4 (over z), tp: 2 (over x), dp: 2 (over core).
Axes of the slice: x: 2, y: 2, z: 4, core: 2. Of those that a mesh axis runs over, the one named last changes fastest.
Arguments:
- tokens: bfloat16 [1024, 5120], P(('groups', 'ctx'), ('tp', 'dp')), parts along dimension 0, may hold values from -6 to 6
- lengths: int32 [8], P('groups'), parts along dimension 0, may hold values from 1 to 256, 512 in all
- request_adapter_ids: int32 [8], P('groups'), parts along dimension 0, may hold values from 0 to 7
- adapter_store_slot: int32 [8], replicated, may hold values from 0 to 7, each once
- xchan_input_weight: bfloat16 [5120, 4096], P('ctx', ('tp', 'dp')), may hold values from -0.078125 to 0.078125
- bc_input_weight: bfloat16 [5120, 512], P('ctx', ('tp', 'dp')), may hold values from -0.078125 to 0.078125
- step_input_weight: bfloat16 [5120, 64], P('ctx', ('tp', 'dp')), may hold values from -0.078125 to 0.078125
- convolution_x_taps: float32 [4, 4096], P(None, ('tp', 'dp')), may hold values from -3 to 3
- convolution_bc_taps: float32 [4, 512], P(None, ('tp', 'dp')), may hold values from -3 to 3
- step_bias: float32 [64], P(('tp', 'dp')), may hold values from -2 to 1
- decay_log_rate: float32 [64], P(('tp', 'dp')), may hold values from -16 to -2
- head_skip_gain: float32 [64], P(('tp', 'dp')), may hold values from 0.5 to 1.5
- output_norm_gain: float32 [4096], P(('tp', 'dp')), may hold values from 0.1 to 1.9
- output_weight: bfloat16 [4096, 5120], P(('tp', 'dp'), 'ctx'), may hold values from -0.09375 to 0.09375
- adapter_down_input: bfloat16 [8, 5120, 64], P('ctx', ('tp', 'dp')), may hold values from -0.078125 to 0.078125
- adapter_up_xchan: bfloat16 [8, 64, 4096], P('ctx', None, ('tp', 'dp')), may hold values from -0.75 to 0.75
- adapter_up_bc: bfloat16 [8, 64, 512], P('ctx', None, ('tp', 'dp')), may hold values from -0.75 to 0.75
- adapter_down_output: bfloat16 [8, 4096, 64], P('ctx', ('tp', 'dp')), may hold values from -0.09375 to 0.09375
- adapter_up_output: bfloat16 [8, 64, 5120], P('ctx', None, ('tp', 'dp')), may hold values from -0.75 to 0.75
Outputs:
- mixed: bfloat16 [1024, 5120], P(('groups', 'ctx'), ('tp', 'dp')), parts along dimension 0
There are 2 independent parts, one for each index of `groups`. A program takes and returns all parts, laid end to end along the dimension named above; an argument that names none is the same for every part. Nothing has to cross between parts.
Inputs may be any that keep to these rules, and one draw needn't show every extreme that they name: The 4 lengths add up to 512; the longest is exactly 256. `adapter_store_slot`: each slot once; the adapter in slot k is stored on index k // 2 of ctx, at its place k % 2 there.
All inputs are finite; a program needn't handle non-finite values.
Results may differ from a plain program's by a relative error of at most 0.023.
Values may be sent and summed in bfloat16 or wider, within the bound.
No kernel may reach another device: no remote copies, remote signals or barrier semaphores. Data moves between devices by JAX's collectives and lax.ppermute only.
A program may use at most 64 MiB of HBM per device.

v0:
```python
import jax
import jax.numpy as jnp
from jax import lax
from jax.sharding import PartitionSpec as P

FULL_PRECISION = lax.Precision.HIGHEST
NORM_EPSILON = 1e-06


def from_root(block, axis, source):
    block = jnp.where(lax.axis_index(axis) == source, block, jnp.zeros_like(block))
    return lax.psum(block, axis)


def passed_along(shard, axis, by):
    size = lax.axis_size(axis)
    pairs = [(i, i + by) for i in range(size) if 0 <= i + by < size]
    return lax.ppermute(shard, axis, pairs)


def prefix(shard, axis, combine, identity):
    size, place = (lax.axis_size(axis), lax.axis_index(axis))
    everything = jax.tree.map(
        lambda part, kind: lax.all_gather(part.astype(kind), axis),
        shard,
        (jnp.bfloat16, jnp.bfloat16),
    )
    start = jax.tree.map(
        lambda part, zero: jnp.broadcast_to(jnp.asarray(zero, part.dtype), part.shape),
        shard,
        identity,
    )

    def lap(k, before):
        reached = k < place
        new = combine(
            before, jax.tree.map(lambda part, own: part[k].astype(own.dtype), everything, shard)
        )
        return jax.tree.map(lambda a, b: jnp.where(reached, a, b), new, before)

    return lax.fori_loop(0, size, lap, start)


def segment_of(positions, request_ends):
    inside = (positions[:, None] >= request_ends[None, :]).astype(jnp.int32)
    counted = jnp.sum(inside, axis=1, dtype=jnp.int32)
    return jnp.where(positions < 0, jnp.int32(-1), counted)


def span_parts(x_heads, b_proj, c_proj, step_size, log_decay, segment, previous):
    length = x_heads.shape[0]
    cumulative = jnp.cumsum(log_decay, axis=0)
    final_log = cumulative[length - 1]
    places = jnp.arange(length, dtype=jnp.int32)
    same_request = jnp.logical_and(
        segment[:, None] == segment[None, :], places[None, :] <= places[:, None]
    ).astype(jnp.float32)
    log_gap = cumulative.T[:, :, None] - cumulative.T[:, None, :]
    decay_table = jnp.exp(jnp.minimum(log_gap, 0.0)) * same_request[None]
    scores = lax.dot_general(
        c_proj, b_proj, (((1,), (1,)), ((), ())), preferred_element_type=jnp.float32
    )
    weights = scores[None] * decay_table * step_size.T[:, None, :]
    inner_out = jnp.einsum("hts,shd->thd", weights, x_heads, precision=FULL_PRECISION)
    at_end = (segment == segment[length - 1]).astype(jnp.float32)
    state_weight = jnp.exp(final_log[None, :] - cumulative) * at_end[:, None] * step_size
    local_state = jnp.einsum(
        "sh,shd,sn->hdn",
        state_weight,
        x_heads,
        b_proj.astype(jnp.float32),
        precision=FULL_PRECISION,
    )
    enter_weight = jnp.exp(cumulative) * (segment == previous).astype(jnp.float32)[:, None]
    carry_decay = jnp.exp(final_log) * (segment[length - 1] == previous).astype(jnp.float32)
    return (inner_out, local_state, enter_weight, carry_decay)


def select_rows(wide, adapter_picker_matrix):
    shaped = wide.reshape(wide.shape[0], adapter_picker_matrix.shape[1], -1)
    return jnp.sum(shaped * adapter_picker_matrix[:, :, None], axis=1)


def masked_wide(values, onehot_b):
    return (values[:, None, :] * onehot_b[:, :, None]).reshape(values.shape[0], -1)


def body(
    tokens,
    lengths,
    request_adapter_ids,
    adapter_store_slot,
    xchan_input_weight,
    bc_input_weight,
    step_input_weight,
    convolution_x_taps,
    convolution_bc_taps,
    step_bias,
    decay_log_rate,
    head_skip_gain,
    output_norm_gain,
    output_weight,
    adapter_down_input,
    adapter_up_xchan,
    adapter_up_bc,
    adapter_down_output,
    adapter_up_output,
):
    length = tokens.shape[0]
    request_list = lengths.shape[0]
    taps = convolution_x_taps.shape[0]
    bank_entries = adapter_down_input.shape[0]
    head_count = step_bias.shape[0]
    channels = xchan_input_weight.shape[1]
    start_pos = lax.axis_index("ctx") * length
    request_ends = jnp.cumsum(lengths, dtype=jnp.int32)
    positions = start_pos + jnp.arange(length, dtype=jnp.int32)
    segment = segment_of(positions, request_ends)
    previous = segment_of(jnp.reshape(start_pos - 1, (1,)), request_ends)[0]
    adapter_picker_matrix = (
        segment[:, None] == jnp.arange(request_list, dtype=jnp.int32)[None, :]
    ).astype(jnp.float32)
    onehot_b = adapter_picker_matrix.astype(jnp.bfloat16)
    slot_indices = adapter_store_slot[request_adapter_ids]
    initial_stacks = (
        jnp.zeros(
            (adapter_down_input.shape[1], request_list, adapter_down_input.shape[2]), jnp.bfloat16
        ),
        jnp.zeros((request_list,) + adapter_up_xchan.shape[1:], jnp.bfloat16),
        jnp.zeros((request_list,) + adapter_up_bc.shape[1:], jnp.bfloat16),
        jnp.zeros(
            (adapter_down_output.shape[1], request_list, adapter_down_output.shape[2]), jnp.bfloat16
        ),
        jnp.zeros((request_list,) + adapter_up_output.shape[1:], jnp.bfloat16),
    )
    stack_dims = (1, 0, 0, 1, 0)

    def fetch(request_item, current):
        slot = slot_indices[request_item]
        owner = slot // bank_entries
        within = slot % bank_entries
        a_in, b_x, b_bc, a_out, b_out = [
            lax.dynamic_index_in_dim(adapter_bank, within, 0, keepdims=False)
            for adapter_bank in (
                adapter_down_input,
                adapter_up_xchan,
                adapter_up_bc,
                adapter_down_output,
                adapter_up_output,
            )
        ]
        received = (
            from_root(a_in, "ctx", owner),
            from_root(b_x, "ctx", owner),
            from_root(b_bc, "ctx", owner),
            from_root(a_out, "ctx", owner),
            from_root(b_out, "ctx", owner),
        )
        return tuple(
            (
                lax.dynamic_update_index_in_dim(stack, panel, request_item, along)
                for stack, panel, along in zip(current, received, stack_dims)
            )
        )

    stacks = lax.fori_loop(0, request_list, fetch, initial_stacks)
    rank_value = adapter_down_input.shape[2]
    down_in = stacks[0].reshape(stacks[0].shape[0], request_list * rank_value)
    up_x = stacks[1].reshape(request_list * rank_value, -1)
    up_bc = stacks[2].reshape(request_list * rank_value, -1)
    down_out = stacks[3].reshape(stacks[3].shape[0], request_list * rank_value)
    up_out = stacks[4].reshape(request_list * rank_value, -1)
    lowrank_part = select_rows(
        jnp.dot(tokens, down_in, preferred_element_type=jnp.float32), adapter_picker_matrix
    )
    rank_hidden = lax.psum(lowrank_part.astype(jnp.bfloat16), ("tp", "dp"))
    lowrank_wide = masked_wide(rank_hidden, onehot_b)
    full_tokens = lax.all_gather(tokens, ("tp", "dp"), axis=1, tiled=True)
    pieces = (
        lax.all_gather(xchan_input_weight, "ctx", axis=0, tiled=True),
        lax.all_gather(bc_input_weight, "ctx", axis=0, tiled=True),
        lax.all_gather(step_input_weight, "ctx", axis=0, tiled=True),
    )
    xchan_values, bc_channel_values, step_raw = tuple(
        (jnp.dot(full_tokens, piece, preferred_element_type=jnp.float32) for piece in pieces)
    )
    xchan_values = xchan_values + jnp.dot(lowrank_wide, up_x, preferred_element_type=jnp.float32)
    bc_channel_values = bc_channel_values + jnp.dot(
        lowrank_wide, up_bc, preferred_element_type=jnp.float32
    )
    values = jnp.concatenate([xchan_values, bc_channel_values], axis=1)
    kernel = jnp.concatenate([convolution_x_taps, convolution_bc_taps], axis=1)
    tail_rows = passed_along(values[length - (taps - 1) :], "ctx", 1)
    extended = jnp.concatenate([tail_rows, values], axis=0)
    extended_segment = segment_of(
        start_pos - (taps - 1) + jnp.arange(length + taps - 1, dtype=jnp.int32), request_ends
    )
    convolved = jnp.zeros_like(values)
    for tap in range(taps):
        keep = (extended_segment[tap : tap + length] == segment).astype(jnp.float32)
        convolved = convolved + kernel[tap][None, :] * extended[tap : tap + length] * keep[:, None]
    act = jax.nn.silu(convolved)
    x_heads = act[:, :channels].reshape(length, head_count, -1)
    bc_local = act[:, channels:].astype(jnp.bfloat16)
    bc_all = lax.all_gather(bc_local, ("tp", "dp"), axis=1, tiled=True)
    state_width = bc_all.shape[1] // 2
    b_proj = bc_all[:, :state_width]
    c_proj = bc_all[:, state_width:]
    step_size = jax.nn.softplus(step_raw + step_bias[None, :])
    log_decay = -step_size * jnp.exp(decay_log_rate)[None, :]
    inner_out, local_state, enter_weight, carry_decay = span_parts(
        x_heads, b_proj, c_proj, step_size, log_decay, segment, previous
    )

    def compose(earlier, later):
        return (earlier[0] * later[0], later[0][:, None, None] * earlier[1] + later[1])

    carried = prefix(
        (carry_decay, local_state),
        "ctx",
        compose,
        (jnp.ones_like(carry_decay), jnp.zeros_like(local_state)),
    )
    entering = carried[1]
    entered = (
        jnp.einsum("tn,hdn->thd", c_proj.astype(jnp.float32), entering, precision=FULL_PRECISION)
        * enter_weight[:, :, None]
    )
    mixer_out = (inner_out + entered + head_skip_gain[None, :, None] * x_heads).reshape(
        length, channels
    )
    scale = lax.rsqrt(jnp.mean(mixer_out * mixer_out, axis=1, keepdims=True) + NORM_EPSILON)
    normalized_rows = (mixer_out * scale * output_norm_gain[None, :]).astype(jnp.bfloat16)
    term = jnp.dot(
        normalized_rows,
        lax.all_gather(output_weight, "ctx", axis=1, tiled=True),
        preferred_element_type=jnp.float32,
    )
    base = lax.psum_scatter(
        term.astype(jnp.bfloat16), ("tp", "dp"), scatter_dimension=1, tiled=True
    ).astype(jnp.float32)
    lowrank_out_part = select_rows(
        jnp.dot(normalized_rows, down_out, preferred_element_type=jnp.float32),
        adapter_picker_matrix,
    )
    rank_hidden_output = lax.psum(lowrank_out_part.astype(jnp.bfloat16), ("tp", "dp"))
    adapter_term = jnp.dot(
        masked_wide(rank_hidden_output, onehot_b), up_out, preferred_element_type=jnp.float32
    )
    return (base + adapter_term).astype(jnp.bfloat16)


def solution(mesh):
    placed = (
        P(("groups", "ctx"), ("tp", "dp")),
        P("groups"),
        P("groups"),
        P(),
        P("ctx", ("tp", "dp")),
        P("ctx", ("tp", "dp")),
        P("ctx", ("tp", "dp")),
        P(None, ("tp", "dp")),
        P(None, ("tp", "dp")),
        P(("tp", "dp")),
        P(("tp", "dp")),
        P(("tp", "dp")),
        P(("tp", "dp")),
        P(("tp", "dp"), "ctx"),
        P("ctx", ("tp", "dp"), None),
        P("ctx", None, ("tp", "dp")),
        P("ctx", None, ("tp", "dp")),
        P("ctx", ("tp", "dp"), None),
        P("ctx", None, ("tp", "dp")),
    )
    return jax.shard_map(
        body,
        mesh=mesh,
        in_specs=placed,
        out_specs=P(("groups", "ctx"), ("tp", "dp")),
        check_vma=False,
    )
```

profile of v0, /device:TPU:0, one launch (start us, length us, event | category | flops | bytes accessed | tf_op | source)
XLA Modules:
  0.0 752.0 jit_solution(9867855290832250756)
XLA Ops:
  8.7 217.9 %while.37 = (s32[]{:T(128)}, bf16[1280,4,64]{0,2,1:T(8,128)(2,1)S(1)}, bf16[4,64,1024]{2,1,0:T(8,128)(2,1)S(1)}, bf16[4,64,128]{2,1,0:T(8,128)(2,1)S(1)}, bf16[1...) while((s32[]{:T(128)}, ...), condition=%wide.region_6.7_spmd, body=%wide.region_0.6_spmd.sunk | while | flops 606236 | bytes 6128176 | solution.py:166
  11.9 1.6 dynamic-slice_select_fusion.7
  13.5 1.6 select_bitcast_fusion.4
  15.1 1.6 dynamic-slice_select_fusion.6
  16.7 1.6 select_bitcast_fusion.5
  18.3 20.5 %psum.87 = bf16[1,64,128]{2,1,0:T(8,128)(2,1)S(1)} all-reduce(bf16[1,64,128]{2,1,0:T(8,128)(2,1)S(1)} %dynamic-slice_select_fusion.8), channel_id=1, replica_groups=mesh['groups'=2,'ctx'=4,'tp'=2,'dp'=2] {'ctx'}, use_global_device_ids=true, to_apply=%region_3.3 | all-reduce | flops 8192 | bytes 32768 | tf_op jit(solution)/shard_map/while/body/eval_jaxpr/psum | solution.py:12
  38.8 22.3 %all-reduce.5.cloned.1.call-done = (bf16[1280,1,64]{0,2,1:T(8,128)(2,1)}, bf16[1,64,1024]{2,1,0:T(8,128)(2,1)}, bf16[1024,1,64]{0,2,1:T(8,128)(2,1)}, bf16[1,64,1280]{2,1,0:T(8,128)(2,1)}) async-done(((bf16[1280,1,64]{0,2,1:T(8,128)(2,1)}, bf16[1,64,1024]{2,1,0:T(8,128)(2,1)}, bf16[1024,1,64]{0,2,1:T(8,128)(2,1)}, bf16[1,64,1280]{2,1,0:T(8,128)(2,1)}), (bf16[1280,1,64]{0,2,1:T(8,128)(2,1)}, ...) | async-done | bytes 589840 | tf_op jit(solution)/shard_map/while/body/eval_jaxpr/psum | solution.py:12
  63.9 1.6 constant_dynamic-update-slice_fusion.15
  68.7 1.6 dynamic-slice_select_fusion.7
  70.3 1.6 select_bitcast_fusion.4
  71.9 1.6 dynamic-slice_select_fusion.6
  73.5 1.6 select_bitcast_fusion.5
  75.1 17.3 %psum.87 = bf16[1,64,128]{2,1,0:T(8,128)(2,1)S(1)} all-reduce(bf16[1,64,128]{2,1,0:T(8,128)(2,1)S(1)} %dynamic-slice_select_fusion.8), channel_id=1, replica_groups=mesh['groups'=2,'ctx'=4,'tp'=2,'dp'=2] {'ctx'}, use_global_device_ids=true, to_apply=%region_3.3 | all-reduce | flops 8192 | bytes 32768 | tf_op jit(solution)/shard_map/while/body/eval_jaxpr/psum | solution.py:12
  92.4 22.4 %all-reduce.5.cloned.1.call-done = (bf16[1280,1,64]{0,2,1:T(8,128)(2,1)}, bf16[1,64,1024]{2,1,0:T(8,128)(2,1)}, bf16[1024,1,64]{0,2,1:T(8,128)(2,1)}, bf16[1,64,1280]{2,1,0:T(8,128)(2,1)}) async-done(((bf16[1280,1,64]{0,2,1:T(8,128)(2,1)}, bf16[1,64,1024]{2,1,0:T(8,128)(2,1)}, bf16[1024,1,64]{0,2,1:T(8,128)(2,1)}, bf16[1,64,1280]{2,1,0:T(8,128)(2,1)}), (bf16[1280,1,64]{0,2,1:T(8,128)(2,1)}, ...) | async-done | bytes 589840 | tf_op jit(solution)/shard_map/while/body/eval_jaxpr/psum | solution.py:12
  117.6 1.6 constant_dynamic-update-slice_fusion.15
  122.4 1.6 dynamic-slice_select_fusion.7
  124.0 1.6 select_bitcast_fusion.4
  125.6 1.6 dynamic-slice_select_fusion.6
  127.2 1.6 select_bitcast_fusion.5
  128.8 17.3 %psum.87 = bf16[1,64,128]{2,1,0:T(8,128)(2,1)S(1)} all-reduce(bf16[1,64,128]{2,1,0:T(8,128)(2,1)S(1)} %dynamic-slice_select_fusion.8), channel_id=1, replica_groups=mesh['groups'=2,'ctx'=4,'tp'=2,'dp'=2] {'ctx'}, use_global_device_ids=true, to_apply=%region_3.3 | all-reduce | flops 8192 | bytes 32768 | tf_op jit(solution)/shard_map/while/body/eval_jaxpr/psum | solution.py:12
  146.1 22.4 %all-reduce.5.cloned.1.call-done = (bf16[1280,1,64]{0,2,1:T(8,128)(2,1)}, bf16[1,64,1024]{2,1,0:T(8,128)(2,1)}, bf16[1024,1,64]{0,2,1:T(8,128)(2,1)}, bf16[1,64,1280]{2,1,0:T(8,128)(2,1)}) async-done(((bf16[1280,1,64]{0,2,1:T(8,128)(2,1)}, bf16[1,64,1024]{2,1,0:T(8,128)(2,1)}, bf16[1024,1,64]{0,2,1:T(8,128)(2,1)}, bf16[1,64,1280]{2,1,0:T(8,128)(2,1)}), (bf16[1280,1,64]{0,2,1:T(8,128)(2,1)}, ...) | async-done | bytes 589840 | tf_op jit(solution)/shard_map/while/body/eval_jaxpr/psum | solution.py:12
  171.3 1.6 constant_dynamic-update-slice_fusion.15
  176.1 1.6 dynamic-slice_select_fusion.7
  177.7 1.6 select_bitcast_fusion.4
  179.3 1.6 dynamic-slice_select_fusion.6
  180.8 1.6 select_bitcast_fusion.5
  182.5 17.3 %psum.87 = bf16[1,64,128]{2,1,0:T(8,128)(2,1)S(1)} all-reduce(bf16[1,64,128]{2,1,0:T(8,128)(2,1)S(1)} %dynamic-slice_select_fusion.8), channel_id=1, replica_groups=mesh['groups'=2,'ctx'=4,'tp'=2,'dp'=2] {'ctx'}, use_global_device_ids=true, to_apply=%region_3.3 | all-reduce | flops 8192 | bytes 32768 | tf_op jit(solution)/shard_map/while/body/eval_jaxpr/psum | solution.py:12
  199.8 22.4 %all-reduce.5.cloned.1.call-done = (bf16[1280,1,64]{0,2,1:T(8,128)(2,1)}, bf16[1,64,1024]{2,1,0:T(8,128)(2,1)}, bf16[1024,1,64]{0,2,1:T(8,128)(2,1)}, bf16[1,64,1280]{2,1,0:T(8,128)(2,1)}) async-done(((bf16[1280,1,64]{0,2,1:T(8,128)(2,1)}, bf16[1,64,1024]{2,1,0:T(8,128)(2,1)}, bf16[1024,1,64]{0,2,1:T(8,128)(2,1)}, bf16[1,64,1280]{2,1,0:T(8,128)(2,1)}), (bf16[1280,1,64]{0,2,1:T(8,128)(2,1)}, ...) | async-done | bytes 589840 | tf_op jit(solution)/shard_map/while/body/eval_jaxpr/psum | solution.py:12
  225.0 1.6 constant_dynamic-update-slice_fusion.15
  231.5 11.7 %psum.84 = bf16[128,64]{0,1:T(8,128)(2,1)S(1)} all-reduce(bf16[128,64]{0,1:T(8,128)(2,1)S(1)} %multiply_reduce_fusion.1), channel_id=1, replica_groups=mesh['groups'=2,'ctx'=4,'tp'=2,'dp'=2] {'tp','dp'}, use_global_device_ids=true, to_apply=%region_10.11 | all-reduce | flops 8192 | bytes 32768 | tf_op jit(solution)/shard_map/psum | solution.py:176
  243.2 13.8 %all_gather.32 = bf16[5120,16]{0,1:T(8,128)(2,1)S(1)} all-gather(bf16[1280,16]{0,1:T(8,128)(2,1)S(1)} %copy-done.5), channel_id=1, replica_groups=mesh['groups'=2,'ctx'=4,'tp'=2,'dp'=2] {'ctx'}, dimensions={0}, use_global_device_ids=true | all-gather | bytes 204800 | tf_op jit(solution)/shard_map/all_gather | solution.py:182
  258.3 1.9 compare_select_fusion
  260.6 19.5 %all-gather.12.cloned.1.call-done = bf16[5120,128]{1,0:T(8,128)(2,1)} async-done(((bf16[1280,128]{1,0:T(8,128)(2,1)}), bf16[5120,128]{1,0:T(8,128)(2,1)}) %all-gather.12.cloned.1.call-update) | async-done | bytes 1310736 | tf_op jit(solution)/shard_map/all_gather | solution.py:181
  280.1 1.8 convolution_add_fusion.1
  282.0 182.5 %all-gather.10.cloned.1.call-done = bf16[5120,1024]{1,0:T(8,128)(2,1)} async-done(((bf16[1280,1024]{1,0:T(8,128)(2,1)}), bf16[5120,1024]{1,0:T(8,128)(2,1)}) %all-gather.10.cloned.1.call-update) | async-done | bytes 10485776 | tf_op jit(solution)/shard_map/all_gather | solution.py:180
  464.5 5.6 convolution_add_fusion
  471.5 1.4 collective-permute-done
  473.6 5.4 all_gather.31
  479.1 1.4 convolution_convert_fusion.1
  481.4 10.7 %all-gather.1 = bf16[4,1,16]{2,1,0:T(2,128)(2,1)S(1)} all-gather(bf16[1,1,16]{2,1,0:T(2,128)(2,1)S(1)} %get-tuple-element.473), channel_id=1, replica_groups=mesh['groups'=2,'ctx'=4,'tp'=2,'dp'=2] {'ctx'}, dimensions={0}, use_global_device_ids=true | all-gather | bytes 160 | tf_op jit(solution)/shard_map/all_gather | solution.py:24
  492.5 2.3 convolution_bitcast_fusion.1
  494.8 32.5 %all-gather.16.cloned.1.call-done = bf16[64,64,256]{2,1,0:T(8,128)(2,1)} async-done(((bf16[16,64,256]{2,1,0:T(8,128)(2,1)}), bf16[64,64,256]{2,1,0:T(8,128)(2,1)}) %all-gather.16.cloned.1.call-update) | async-done | bytes 2097168 | tf_op jit(solution)/shard_map/all_gather | solution.py:24
  527.3 5.4 while.38
  533.5 177.9 %all-gather.14.cloned.1.call-done = bf16[1024,5120]{1,0:T(8,128)(2,1)} async-done(((bf16[1024,1280]{1,0:T(8,128)(2,1)}), bf16[1024,5120]{1,0:T(8,128)(2,1)}) %all-gather.14.cloned.1.call-update) | async-done | bytes 10485776 | tf_op jit(solution)/shard_map/all_gather | solution.py:236
  711.5 6.6 convolution_convert_fusion
  719.4 11.2 %psum.85 = bf16[128,64]{0,1:T(8,128)(2,1)S(1)} all-reduce(bf16[128,64]{0,1:T(8,128)(2,1)S(1)} %fusion.5), channel_id=1, replica_groups=mesh['groups'=2,'ctx'=4,'tp'=2,'dp'=2] {'tp','dp'}, use_global_device_ids=true, to_apply=%region_19.20 | all-reduce | flops 8192 | bytes 32768 | tf_op jit(solution)/shard_map/psum | solution.py:246
  730.6 12.3 %reduce-scatter.2.cloned.1.call-done = bf16[128,1280]{1,0:T(8,128)(2,1)} async-done(((bf16[128,5120]{1,0:T(8,128)(2,1)}), bf16[128,1280]{1,0:T(8,128)(2,1)}) %reduce-scatter.2.cloned.1.call-update) | async-done | bytes 327696 | tf_op jit(solution)/shard_map/reduce_scatter | solution.py:239
  742.9 2.0 fusion.2
  (138 shorter events, 31.1 us)
Async XLA Ops:
  7.4 0.7 copy-start
  8.7 9.6 %copy-start.4 = (bf16[2,64,128]{2,1,0:T(8,128)(2,1)S(1)}, bf16[2,64,128]{2,1,0:T(8,128)(2,1)}, u32[]{:S(2)}) copy-start(bf16[2,64,128]{2,1,0:T(8,128)(2,1)} %get-tuple-element.642) | copy-start | bytes 98308 | tf_op jit(solution)/shard_map/while
  8.7 52.5 %all-reduce.5.cloned.1.call-start = ((), (), s32[]{:S(2)}) async-start(), calls=%async_computation.7 | async-start | bytes 1179648 | tf_op jit(solution)/shard_map/while/body/eval_jaxpr/psum | solution.py:12
  65.5 9.5 %copy-start.4 = (bf16[2,64,128]{2,1,0:T(8,128)(2,1)S(1)}, bf16[2,64,128]{2,1,0:T(8,128)(2,1)}, u32[]{:S(2)}) copy-start(bf16[2,64,128]{2,1,0:T(8,128)(2,1)} %get-tuple-element.642) | copy-start | bytes 98308 | tf_op jit(solution)/shard_map/while
  65.5 49.3 %all-reduce.5.cloned.1.call-start = ((), (), s32[]{:S(2)}) async-start(), calls=%async_computation.7 | async-start | bytes 1179648 | tf_op jit(solution)/shard_map/while/body/eval_jaxpr/psum | solution.py:12
  119.2 9.5 %copy-start.4 = (bf16[2,64,128]{2,1,0:T(8,128)(2,1)S(1)}, bf16[2,64,128]{2,1,0:T(8,128)(2,1)}, u32[]{:S(2)}) copy-start(bf16[2,64,128]{2,1,0:T(8,128)(2,1)} %get-tuple-element.642) | copy-start | bytes 98308 | tf_op jit(solution)/shard_map/while
  119.2 49.3 %all-reduce.5.cloned.1.call-start = ((), (), s32[]{:S(2)}) async-start(), calls=%async_computation.7 | async-start | bytes 1179648 | tf_op jit(solution)/shard_map/while/body/eval_jaxpr/psum | solution.py:12
  172.9 9.5 %copy-start.4 = (bf16[2,64,128]{2,1,0:T(8,128)(2,1)S(1)}, bf16[2,64,128]{2,1,0:T(8,128)(2,1)}, u32[]{:S(2)}) copy-start(bf16[2,64,128]{2,1,0:T(8,128)(2,1)} %get-tuple-element.642) | copy-start | bytes 98308 | tf_op jit(solution)/shard_map/while
  172.9 49.3 %all-reduce.5.cloned.1.call-start = ((), (), s32[]{:S(2)}) async-start(), calls=%async_computation.7 | async-start | bytes 1179648 | tf_op jit(solution)/shard_map/while/body/eval_jaxpr/psum | solution.py:12
  226.6 31.7 %all-gather.8.cloned.1.call-start = ((), (), s32[]{:S(2)}) async-start(), calls=%async_computation.1 | async-start | bytes 1638400 | tf_op jit(solution)/shard_map/all_gather | solution.py:178
  227.1 53.0 %all-gather.12.cloned.1.call-start = ((), (), s32[]{:S(2)}) async-start(), calls=%async_computation.3 | async-start | bytes 1638400 | tf_op jit(solution)/shard_map/all_gather | solution.py:181
  227.7 0.7 copy-start.11
  227.7 3.4 copy-start.12
  227.7 3.4 copy-start.2
  227.8 236.7 %all-gather.10.cloned.1.call-start = ((), (), s32[]{:S(2)}) async-start(), calls=%async_computation.2 | async-start | bytes 13107200 | tf_op jit(solution)/shard_map/all_gather | solution.py:180
  228.3 14.9 %copy-start.5 = (bf16[1280,16]{0,1:T(8,128)(2,1)S(1)}, bf16[1280,16]{0,1:T(8,128)(2,1)}, u32[]{:S(2)}) copy-start(bf16[1280,16]{0,1:T(8,128)(2,1)} %param.29) | copy-start | bytes 122884
  228.3 28.7 %copy-start.7 = (f32[4,1024]{1,0:T(4,128)S(1)}, f32[4,1024]{1,0:T(4,128)}, u32[]{:S(2)}) copy-start(f32[4,1024]{1,0:T(4,128)} %param.30) | copy-start | bytes 49156
  228.4 28.7 %copy-start.8 = (f32[4,128]{1,0:T(4,128)S(1)}, f32[4,128]{1,0:T(4,128)}, u32[]{:S(2)}) copy-start(f32[4,128]{1,0:T(4,128)} %param.31) | copy-start | bytes 6148
  228.4 298.9 %all-gather.16.cloned.1.call-start = ((), (), s32[]{:S(2)}) async-start(), calls=%async_computation.6 | async-start | bytes 2621440 | tf_op jit(solution)/shard_map/all_gather | solution.py:24
  231.1 27.2 %copy-start.9 = (f32[16]{0:T(128)S(1)}, f32[16]{0:T(128)}, u32[]{:S(2)}) copy-start(f32[16]{0:T(128)} %param.32) | copy-start | bytes 196
  258.3 21.8 %copy-start.1 = (bf16[128,5120]{1,0:T(8,128)(2,1)S(1)}, bf16[128,5120]{1,0:T(8,128)(2,1)}, u32[]{:S(2)}) copy-start(bf16[128,5120]{1,0:T(8,128)(2,1)} %all-gather.8.cloned.1.call-done) | copy-start | bytes 3932164
  470.1 2.7 collective-permute-start
  480.5 231.0 %all-gather.14.cloned.1.call-start = ((), (), s32[]{:S(2)}) async-start(), calls=%async_computation.4 | async-start | bytes 13107200 | tf_op jit(solution)/shard_map/all_gather | solution.py:236
  481.3 261.6 %reduce-scatter.2.cloned.1.call-start = ((), (), s32[]{:S(2)}) async-start(), calls=%async_computation.5 | async-start | bytes 1638400 | tf_op jit(solution)/shard_map/reduce_scatter | solution.py:239
  527.3 5.4 copy-start.10
  532.6 0.7 copy-start.6
  718.1 1.0 copy-start.3
Sparse Core Ops, SparseCore 0:
  18.4 42.7 all-reduce.4
  75.2 39.6 all-reduce.4
  128.9 39.6 all-reduce.4
  182.5 39.6 all-reduce.4
Sparse Core Ops, SparseCore 1:
  228.6 17.6 all-gather.7
  247.7 32.4 all-gather.11
  281.6 182.8 all-gather.9
  480.6 46.6 all-gather.15
  528.9 182.5 all-gather.13
  718.2 24.6 reduce-scatter.1
where the time goes:
time: 754 us; the launch traced here: 752 us
  waiting for transfers between devices  518 us (69%)
  blocking collectives  125 us (17%)
  other arithmetic  34.3 us (5%)
  matrix products  23.5 us (3%)
  local copies, waits for them, and re-layouts  22.5 us (3%)
  between operations  16.1 us (2%)
  loops' own time  10.7 us (1%)
    all_gather x1, waiting for transfers between devices, body(): lax.all_gather(xchan_input_weight, 'ctx', axis=0, tiled=True)  182 us
    all_gather x1, waiting for transfers between devices, body(): lax.all_gather(output_weight, 'ctx', axis=1, tiled=True)  178 us
    psum x4, waiting for transfers between devices, from_root(): return lax.psum(block, axis)  89.6 us
    psum x4, blocking collectives, from_root(): return lax.psum(block, axis)  72.5 us
    all_gather x1, waiting for transfers between devices, prefix(): lax.all_gather(part.astype(kind), axis)  32.5 us
    all_gather x1, waiting for transfers between devices, body(): lax.all_gather(bc_input_weight, 'ctx', axis=0, tiled=True)  19.5 us
    dynamic_update_slice x20, local copies, waits for them, and re-layouts, fetch(): lax.dynamic_update_index_in_dim(stack, panel, request_item, along)  17.5 us
  transfers between devices with their start and end apart: 11, of which 10 were waited for; matrix products, arithmetic and copies ran while one was open for 2% of the time, Pallas kernels for 0%

commit v1 on v0

--- a/solution.py
+++ b/solution.py
@@ -5,6 +5,20 @@
 
 FULL_PRECISION = lax.Precision.HIGHEST
 NORM_EPSILON = 1e-06
+
+
+def balance_the_fields(vec):
+    lower, clean = (lax.axis_size("ctx"), lax.axis_index("ctx"))
+    w_next, plain = (vec, 1)
+    while plain < lower:
+        top = lax.ppermute(
+            w_next, axis_name="ctx", perm=tuple(((j, j ^ plain) for j in range(lower)))
+        )
+        part_now = jnp.concatenate([w_next, top], axis=1)
+        a_now = jnp.concatenate([top, w_next], axis=1)
+        w_next = jnp.where(clean & plain == 0, part_now, a_now)
+        plain = 2 * plain
+    return w_next
 
 
 def from_root(block, axis, source):
@@ -232,9 +246,7 @@
     scale = lax.rsqrt(jnp.mean(mixer_out * mixer_out, axis=1, keepdims=True) + NORM_EPSILON)
     normalized_rows = (mixer_out * scale * output_norm_gain[None, :]).astype(jnp.bfloat16)
     term = jnp.dot(
-        normalized_rows,
-        lax.all_gather(output_weight, "ctx", axis=1, tiled=True),
-        preferred_element_type=jnp.float32,
+        normalized_rows, balance_the_fields(output_weight), preferred_element_type=jnp.float32
     )
     base = lax.psum_scatter(
         term.astype(jnp.bfloat16), ("tp", "dp"), scatter_dimension=1, tiled=True

time: 754 us -> 833 us (1.10)
  blocking collectives: 125 us -> 313 us
  waiting for transfers between devices: 518 us -> 387 us
  other arithmetic: 34.3 us -> 47.4 us
    all_gather x1 -> x0, waiting for transfers between devices: 178 us -> none  [body(): lax.all_gather(output_weight, 'ctx', axis=1, tiled=True)]
    all_gather x1, blocking collectives: 10.7 us -> 139 us  [prefix(): lax.all_gather(part.astype(kind), axis)]
    ppermute x0 -> x2, waiting for transfers between devices: none -> 89 us  [balance_the_fields(): lax.ppermute(w_next, axis_name='ctx', perm=tuple(((j, j ^ plain) for j in...]
    all_gather x1, blocking collectives: 13.8 us -> 73.3 us  [body(): lax.all_gather(step_input_weight, 'ctx', axis=0, tiled=True)]
    all_gather x1, waiting for transfers between devices: 182 us -> 163 us  [body(): lax.all_gather(xchan_input_weight, 'ctx', axis=0, tiled=True)]
    all_gather x1, waiting for transfers between devices: 19.5 us -> 0.01 us  [body(): lax.all_gather(bc_input_weight, 'ctx', axis=0, tiled=True)]
    reduce_scatter x1, waiting for transfers between devices: 12.3 us -> 24.5 us  [body(): lax.psum_scatter(term.astype(jnp.bfloat16), ('tp', 'dp'), scatter_dimensi...]
    all_gather x1, waiting for transfers between devices: 32.5 us -> 21.9 us  [prefix(): lax.all_gather(part.astype(kind), axis)]
  transfers between devices with their start and end apart: 11 -> 12, of which waited for: 10 -> 9; matrix products, arithmetic and copies ran while one was open for 2% -> 4% of each run, Pallas kernels for 0% -> 0%
where the time goes in v1:
time: 833 us; the launch traced here: 831 us
  waiting for transfers between devices  387 us (46%)
  blocking collectives  313 us (38%)
  other arithmetic  47.4 us (6%)
  matrix products  28 us (3%)
  local copies, waits for them, and re-layouts  21.7 us (3%)
  between operations  16.4 us (2%)
  loops' own time  10.8 us (1%)
    all_gather x1, waiting for transfers between devices, body(): lax.all_gather(xchan_input_weight, 'ctx', axis=0, tiled=True)  163 us
    all_gather x1, blocking collectives, prefix(): lax.all_gather(part.astype(kind), axis)  139 us
    ppermute x2, waiting for transfers between devices, balance_the_fields(): lax.ppermute(w_next, axis_name='ctx', perm=tuple(((j, j ^ plain) for j in...  89 us
    psum x4, waiting for transfers between devices, from_root(): return lax.psum(block, axis)  85.9 us
    all_gather x1, blocking collectives, body(): lax.all_gather(step_input_weight, 'ctx', axis=0, tiled=True)  73.3 us
    psum x4, blocking collectives, from_root(): return lax.psum(block, axis)  72.9 us
    reduce_scatter x1, waiting for transfers between devices, body(): lax.psum_scatter(term.astype(jnp.bfloat16), ('tp', 'dp'), scatter_dimensi...  24.5 us
    all_gather x1, waiting for transfers between devices, prefix(): lax.all_gather(part.astype(kind), axis)  21.9 us
  transfers between devices with their start and end apart: 12, of which 9 were waited for; matrix products, arithmetic and copies ran while one was open for 4% of the time, Pallas kernels for 0%

profile of v1, /device:TPU:0, one launch (start us, length us, event | category | flops | bytes accessed | tf_op | source)
XLA Modules:
  0.0 831.3 jit_solution(10547791710491602351)
XLA Ops:
  8.7 217.6 %while.37 = (s32[]{:T(128)}, bf16[1280,4,64]{0,2,1:T(8,128)(2,1)S(1)}, bf16[4,64,1024]{2,1,0:T(8,128)(2,1)S(1)}, bf16[4,64,128]{2,1,0:T(8,128)(2,1)S(1)}, bf16[1...) while((s32[]{:T(128)}, ...), condition=%wide.region_6.7_spmd, body=%wide.region_0.6_spmd.sunk | while | flops 606236 | bytes 5997076 | solution.py:180
  12.0 1.6 select_bitcast_fusion.4
  13.6 1.6 dynamic-slice_select_fusion.6
  15.2 1.6 select_bitcast_fusion.5
  16.7 1.6 dynamic-slice_select_fusion.7
  19.1 20.6 %psum.87 = bf16[1,64,128]{2,1,0:T(8,128)(2,1)S(1)} all-reduce(bf16[1,64,128]{2,1,0:T(8,128)(2,1)S(1)} %dynamic-slice_select_fusion.8), channel_id=1, replica_groups=mesh['groups'=2,'ctx'=4,'tp'=2,'dp'=2] {'ctx'}, use_global_device_ids=true, to_apply=%region_3.3 | all-reduce | flops 8192 | bytes 32768 | tf_op jit(solution)/shard_map/while/body/eval_jaxpr/psum | solution.py:26
  39.7 21.5 %all-reduce.5.cloned.1.call-done = (bf16[1280,1,64]{0,2,1:T(8,128)(2,1)}, bf16[1,64,1024]{2,1,0:T(8,128)(2,1)}, bf16[1024,1,64]{0,2,1:T(8,128)(2,1)}, bf16[1,64,1280]{2,1,0:T(8,128)(2,1)}) async-done(((bf16[1280,1,64]{0,2,1:T(8,128)(2,1)}, bf16[1,64,1024]{2,1,0:T(8,128)(2,1)}, bf16[1024,1,64]{0,2,1:T(8,128)(2,1)}, bf16[1,64,1280]{2,1,0:T(8,128)(2,1)}), (bf16[1280,1,64]{0,2,1:T(8,128)(2,1)}, ...) | async-done | bytes 589840 | tf_op jit(solution)/shard_map/while/body/eval_jaxpr/psum | solution.py:26
  63.0 1.6 constant_dynamic-update-slice_fusion.15
  68.8 1.6 select_bitcast_fusion.4
  70.4 1.6 dynamic-slice_select_fusion.6
  72.0 1.6 select_bitcast_fusion.5
  73.5 1.6 dynamic-slice_select_fusion.7
  75.9 17.5 %psum.87 = bf16[1,64,128]{2,1,0:T(8,128)(2,1)S(1)} all-reduce(bf16[1,64,128]{2,1,0:T(8,128)(2,1)S(1)} %dynamic-slice_select_fusion.8), channel_id=1, replica_groups=mesh['groups'=2,'ctx'=4,'tp'=2,'dp'=2] {'ctx'}, use_global_device_ids=true, to_apply=%region_3.3 | all-reduce | flops 8192 | bytes 32768 | tf_op jit(solution)/shard_map/while/body/eval_jaxpr/psum | solution.py:26
  93.3 21.4 %all-reduce.5.cloned.1.call-done = (bf16[1280,1,64]{0,2,1:T(8,128)(2,1)}, bf16[1,64,1024]{2,1,0:T(8,128)(2,1)}, bf16[1024,1,64]{0,2,1:T(8,128)(2,1)}, bf16[1,64,1280]{2,1,0:T(8,128)(2,1)}) async-done(((bf16[1280,1,64]{0,2,1:T(8,128)(2,1)}, bf16[1,64,1024]{2,1,0:T(8,128)(2,1)}, bf16[1024,1,64]{0,2,1:T(8,128)(2,1)}, bf16[1,64,1280]{2,1,0:T(8,128)(2,1)}), (bf16[1280,1,64]{0,2,1:T(8,128)(2,1)}, ...) | async-done | bytes 589840 | tf_op jit(solution)/shard_map/while/body/eval_jaxpr/psum | solution.py:26
  116.6 1.6 constant_dynamic-update-slice_fusion.15
  122.4 1.6 select_bitcast_fusion.4
  124.0 1.6 dynamic-slice_select_fusion.6
  125.6 1.6 select_bitcast_fusion.5
  127.1 1.6 dynamic-slice_select_fusion.7
  129.5 17.5 %psum.87 = bf16[1,64,128]{2,1,0:T(8,128)(2,1)S(1)} all-reduce(bf16[1,64,128]{2,1,0:T(8,128)(2,1)S(1)} %dynamic-slice_select_fusion.8), channel_id=1, replica_groups=mesh['groups'=2,'ctx'=4,'tp'=2,'dp'=2] {'ctx'}, use_global_device_ids=true, to_apply=%region_3.3 | all-reduce | flops 8192 | bytes 32768 | tf_op jit(solution)/shard_map/while/body/eval_jaxpr/psum | solution.py:26
  146.9 21.4 %all-reduce.5.cloned.1.call-done = (bf16[1280,1,64]{0,2,1:T(8,128)(2,1)}, bf16[1,64,1024]{2,1,0:T(8,128)(2,1)}, bf16[1024,1,64]{0,2,1:T(8,128)(2,1)}, bf16[1,64,1280]{2,1,0:T(8,128)(2,1)}) async-done(((bf16[1280,1,64]{0,2,1:T(8,128)(2,1)}, bf16[1,64,1024]{2,1,0:T(8,128)(2,1)}, bf16[1024,1,64]{0,2,1:T(8,128)(2,1)}, bf16[1,64,1280]{2,1,0:T(8,128)(2,1)}), (bf16[1280,1,64]{0,2,1:T(8,128)(2,1)}, ...) | async-done | bytes 589840 | tf_op jit(solution)/shard_map/while/body/eval_jaxpr/psum | solution.py:26
  170.2 1.6 constant_dynamic-update-slice_fusion.15
  176.0 1.6 select_bitcast_fusion.4
  177.6 1.6 dynamic-slice_select_fusion.6
  179.2 1.6 select_bitcast_fusion.5
  180.7 1.6 dynamic-slice_select_fusion.7
  183.1 17.5 %psum.87 = bf16[1,64,128]{2,1,0:T(8,128)(2,1)S(1)} all-reduce(bf16[1,64,128]{2,1,0:T(8,128)(2,1)S(1)} %dynamic-slice_select_fusion.8), channel_id=1, replica_groups=mesh['groups'=2,'ctx'=4,'tp'=2,'dp'=2] {'ctx'}, use_global_device_ids=true, to_apply=%region_3.3 | all-reduce | flops 8192 | bytes 32768 | tf_op jit(solution)/shard_map/while/body/eval_jaxpr/psum | solution.py:26
  200.5 21.4 %all-reduce.5.cloned.1.call-done = (bf16[1280,1,64]{0,2,1:T(8,128)(2,1)}, bf16[1,64,1024]{2,1,0:T(8,128)(2,1)}, bf16[1024,1,64]{0,2,1:T(8,128)(2,1)}, bf16[1,64,1280]{2,1,0:T(8,128)(2,1)}) async-done(((bf16[1280,1,64]{0,2,1:T(8,128)(2,1)}, bf16[1,64,1024]{2,1,0:T(8,128)(2,1)}, bf16[1024,1,64]{0,2,1:T(8,128)(2,1)}, bf16[1,64,1280]{2,1,0:T(8,128)(2,1)}), (bf16[1280,1,64]{0,2,1:T(8,128)(2,1)}, ...) | async-done | bytes 589840 | tf_op jit(solution)/shard_map/while/body/eval_jaxpr/psum | solution.py:26
  223.8 1.6 constant_dynamic-update-slice_fusion.15
  232.6 11.0 %psum.84 = bf16[128,64]{0,1:T(8,128)(2,1)S(1)} all-reduce(bf16[128,64]{0,1:T(8,128)(2,1)S(1)} %multiply_reduce_fusion.1), channel_id=1, replica_groups=mesh['groups'=2,'ctx'=4,'tp'=2,'dp'=2] {'tp','dp'}, use_global_device_ids=true, to_apply=%region_10.11 | all-reduce | flops 8192 | bytes 32768 | tf_op jit(solution)/shard_map/psum | solution.py:190
  243.6 73.3 %all_gather.29 = bf16[5120,16]{0,1:T(8,128)(2,1)S(1)} all-gather(bf16[1280,16]{0,1:T(8,128)(2,1)S(1)} %copy-done.4), channel_id=1, replica_groups=mesh['groups'=2,'ctx'=4,'tp'=2,'dp'=2] {'ctx'}, dimensions={0}, use_global_device_ids=true | all-gather | bytes 204800 | tf_op jit(solution)/shard_map/all_gather | solution.py:196
  318.3 1.9 compare_select_fusion
  320.6 2.2 convolution_add_fusion.1
  322.8 162.9 %all-gather.9.cloned.1.call-done = bf16[5120,1024]{1,0:T(8,128)(2,1)} async-done(((bf16[1280,1024]{1,0:T(8,128)(2,1)}), bf16[5120,1024]{1,0:T(8,128)(2,1)}) %all-gather.9.cloned.1.call-update) | async-done | bytes 10485776 | tf_op jit(solution)/shard_map/all_gather | solution.py:194
  485.8 5.6 convolution_add_fusion
  494.9 5.4 all_gather.28
  500.4 1.4 convolution_convert_fusion
  501.9 8.3 %maximum_select_fusion.4 = bf16[1024,2560]{1,0:T(8,128)(2,1)} fusion(bf16[1024,1280]{1,0:T(8,128)(2,1)} %collective-permute-done.1, bf16[1024,1280]{1,0:T(8,128)(2,1)} %param.36, pred[]{:T(512)S(6)} %eq.116), kind=kLoop, calls=%fused_computation.23 | loop fusion | flops 23592960 | bytes 10485761 | tf_op jit(solution)/shard_map/jit(_where)/select_n | solution.py:19
  510.2 3.5 collective-permute-start.2
  513.8 139.4 %all-gather.1 = bf16[4,1,16]{2,1,0:T(2,128)(2,1)S(1)} all-gather(bf16[1,1,16]{2,1,0:T(2,128)(2,1)S(1)} %get-tuple-element.473), channel_id=1, replica_groups=mesh['groups'=2,'ctx'=4,'tp'=2,'dp'=2] {'ctx'}, dimensions={0}, use_global_device_ids=true | all-gather | bytes 160 | tf_op jit(solution)/shard_map/all_gather | solution.py:38
  653.6 2.3 convolution_bitcast_fusion.1
  655.8 21.9 %all-gather.13.cloned.1.call-done = bf16[64,64,256]{2,1,0:T(8,128)(2,1)} async-done(((bf16[16,64,256]{2,1,0:T(8,128)(2,1)}), bf16[64,64,256]{2,1,0:T(8,128)(2,1)}) %all-gather.13.cloned.1.call-update) | async-done | bytes 2097168 | tf_op jit(solution)/shard_map/all_gather | solution.py:38
  677.8 5.4 while.38
  684.0 89.0 %collective-permute-done.2 = bf16[1024,2560]{1,0:T(8,128)(2,1)} collective-permute-done((bf16[1024,2560]{1,0:T(8,128)(2,1)}, bf16[1024,2560]{1,0:T(8,128)(2,1)}, u32[]{:S(2)}, u32[]{:S(2)}) %collective-permute-start.2) | collective-permute-done | bytes 5242912 | tf_op jit(solution)/shard_map/ppermute | solution.py:14
  773.1 12.5 %fusion.8 = bf16[128,5120]{1,0:T(8,128)(2,1)} fusion(bf16[128,1024]{0,1:T(8,128)(2,1)S(1)} %fusion.28, bf16[1024,2560]{1,0:T(8,128)(2,1)} %collective-permute-done.2, bf16[1024,2560]{1,0:T(8,128)(2,1)} %maximum_select_fusion.4, pred[]{:T(512)S(6)} %eq.115), kind=kOutput, calls=%fused_computation.22 | convolution fusion | flops 1390018560 | bytes 12058625 | tf_op jit(solution)/shard_map/dot_general | solution.py:248
  786.2 11.2 %psum.85 = bf16[128,64]{0,1:T(8,128)(2,1)S(1)} all-reduce(bf16[128,64]{0,1:T(8,128)(2,1)S(1)} %fusion.11), channel_id=1, replica_groups=mesh['groups'=2,'ctx'=4,'tp'=2,'dp'=2] {'tp','dp'}, use_global_device_ids=true, to_apply=%region_19.20 | all-reduce | flops 8192 | bytes 32768 | tf_op jit(solution)/shard_map/psum | solution.py:258
  797.6 24.5 %reduce-scatter.2.cloned.1.call-done = bf16[128,1280]{1,0:T(8,128)(2,1)} async-done(((bf16[128,5120]{1,0:T(8,128)(2,1)}), bf16[128,1280]{1,0:T(8,128)(2,1)}) %reduce-scatter.2.cloned.1.call-update) | async-done | bytes 327696 | tf_op jit(solution)/shard_map/reduce_scatter | solution.py:251
  822.2 1.8 add_convert_fusion
  (133 shorter events, 35.5 us)
Async XLA Ops:
  7.4 0.7 copy-start
  8.7 220.7 %copy-start.10 = (s32[4]{0:T(128)S(1)}, s32[4]{0:T(128)}, u32[]{:S(2)}) copy-start(s32[4]{0:T(128)} %param.24) | copy-start | bytes 52
  8.7 222.8 %copy-start.11 = (f32[16]{0:T(128)S(1)}, f32[16]{0:T(128)}, u32[]{:S(2)}) copy-start(f32[16]{0:T(128)} %param.33) | copy-start | bytes 196
  8.7 223.5 %copy-start.2 = (bf16[128,1280]{1,0:T(8,128)(2,1)S(1)}, bf16[128,1280]{1,0:T(8,128)(2,1)}, u32[]{:S(2)}) copy-start(bf16[128,1280]{1,0:T(8,128)(2,1)} %param.23) | copy-start | bytes 983044
  8.7 234.9 %copy-start.4 = (bf16[1280,16]{0,1:T(8,128)(2,1)S(1)}, bf16[1280,16]{0,1:T(8,128)(2,1)}, u32[]{:S(2)}) copy-start(bf16[1280,16]{0,1:T(8,128)(2,1)} %param.29) | copy-start | bytes 122884
  8.7 308.2 %copy-start.6 = (f32[4,1024]{1,0:T(4,128)S(1)}, f32[4,1024]{1,0:T(4,128)}, u32[]{:S(2)}) copy-start(f32[4,1024]{1,0:T(4,128)} %param.30) | copy-start | bytes 49156
  8.7 308.2 %copy-start.7 = (f32[4,128]{1,0:T(4,128)S(1)}, f32[4,128]{1,0:T(4,128)}, u32[]{:S(2)}) copy-start(f32[4,128]{1,0:T(4,128)} %param.31) | copy-start | bytes 6148
  8.8 52.4 %all-reduce.5.cloned.1.call-start = ((), (), s32[]{:S(2)}) async-start(), calls=%async_computation.6 | async-start | bytes 1179648 | tf_op jit(solution)/shard_map/while/body/eval_jaxpr/psum | solution.py:26
  65.6 49.2 %all-reduce.5.cloned.1.call-start = ((), (), s32[]{:S(2)}) async-start(), calls=%async_computation.6 | async-start | bytes 1179648 | tf_op jit(solution)/shard_map/while/body/eval_jaxpr/psum | solution.py:26
  119.2 49.2 %all-reduce.5.cloned.1.call-start = ((), (), s32[]{:S(2)}) async-start(), calls=%async_computation.6 | async-start | bytes 1179648 | tf_op jit(solution)/shard_map/while/body/eval_jaxpr/psum | solution.py:26
  172.7 49.2 %all-reduce.5.cloned.1.call-start = ((), (), s32[]{:S(2)}) async-start(), calls=%async_computation.6 | async-start | bytes 1179648 | tf_op jit(solution)/shard_map/while/body/eval_jaxpr/psum | solution.py:26
  226.3 92.0 %copy-start.8 = (f32[16]{0:T(128)S(1)}, f32[16]{0:T(128)}, u32[]{:S(2)}) copy-start(f32[16]{0:T(128)} %param.32) | copy-start | bytes 196
  226.3 91.9 %all-gather.7.cloned.1.call-start = ((), (), s32[]{:S(2)}) async-start(), calls=%async_computation.1 | async-start | bytes 1638400 | tf_op jit(solution)/shard_map/all_gather | solution.py:192
  226.9 93.7 %all-gather.11.cloned.1.call-start = ((), (), s32[]{:S(2)}) async-start(), calls=%async_computation.3 | async-start | bytes 1638400 | tf_op jit(solution)/shard_map/all_gather | solution.py:195
  227.5 258.2 %all-gather.9.cloned.1.call-start = ((), (), s32[]{:S(2)}) async-start(), calls=%async_computation.2 | async-start | bytes 13107200 | tf_op jit(solution)/shard_map/all_gather | solution.py:194
  228.1 449.7 %all-gather.13.cloned.1.call-start = ((), (), s32[]{:S(2)}) async-start(), calls=%async_computation.5 | async-start | bytes 2621440 | tf_op jit(solution)/shard_map/all_gather | solution.py:38
  228.1 273.7 %collective-permute-start.1 = (bf16[1024,1280]{1,0:T(8,128)(2,1)}, bf16[1024,1280]{1,0:T(8,128)(2,1)}, u32[]{:S(2)}, u32[]{:S(2)}) collective-permute-start(bf16[1024,1280]{1,0:T(8,128)(2,1)} %param.36), channel_id=1, source_target_pairs={{0,4},{4,0},{8,12},{12,8},{1,5},{5,1},{9,13},{13,9},{2,6},{6,2},{1... | collective-permute-start | bytes 7864328 | tf_op jit(solution)/shard_map/ppermute | solution.py:14
  318.3 167.5 %copy-start.1 = (bf16[128,5120]{1,0:T(8,128)(2,1)S(1)}, bf16[128,5120]{1,0:T(8,128)(2,1)}, u32[]{:S(2)}) copy-start(bf16[128,5120]{1,0:T(8,128)(2,1)} %all-gather.7.cloned.1.call-done) | copy-start | bytes 3932164
  491.4 2.7 collective-permute-start
  501.8 320.4 %reduce-scatter.2.cloned.1.call-start = ((), (), s32[]{:S(2)}) async-start(), calls=%async_computation.4 | async-start | bytes 1638400 | tf_op jit(solution)/shard_map/reduce_scatter | solution.py:251
  510.2 262.9 %collective-permute-start.2 = (bf16[1024,2560]{1,0:T(8,128)(2,1)}, bf16[1024,2560]{1,0:T(8,128)(2,1)}, u32[]{:S(2)}, u32[]{:S(2)}) collective-permute-start(bf16[1024,2560]{1,0:T(8,128)(2,1)} %maximum_select_fusion.4), channel_id=1, source_target_pairs={{0,8},{4,12},{8,0},{12,4},{1,9},{5,13},{9,1},{13,5},{2,10},{6,14},... | collective-permute-start | bytes 15728648 | tf_op jit(solution)/shard_map/ppermute | solution.py:14
  677.8 5.4 copy-start.9
  677.8 6.1 copy-start.5
  684.0 101.8 %copy-start.3 = (bf16[1024,4,64]{0,2,1:T(8,128)(2,1)S(1)}, bf16[1024,4,64]{0,2,1:T(8,128)(2,1)}, u32[]{:S(2)}) copy-start(bf16[1024,4,64]{0,2,1:T(8,128)(2,1)} %get-tuple-element.396) | copy-start | bytes 1572868
Sparse Core Ops, SparseCore 0:
  18.5 42.6 all-reduce.4
  75.3 39.4 all-reduce.4
  128.9 39.4 all-reduce.4
  182.5 39.4 all-reduce.4
Sparse Core Ops, SparseCore 1:
  228.4 17.6 all-gather.6
  247.5 50.3 all-gather.10
  299.3 186.4 all-gather.8
  501.9 175.8 all-gather.12
  785.7 36.4 reduce-scatter.1
